TPU v7x, 32 devices: a whole 2x2x4 slice. The times are simulated.
32 devices in a mesh: groups: 2 (over y), ctx: 4 (over z), head: 2 (over x), rep: 2 (over core).
Axes of the slice: x: 2, y: 2, z: 4, core: 2. Of those that a mesh axis runs over, the one named last changes fastest.
Arguments:
- query: bfloat16 [2048, 4096], P(('groups', 'ctx', 'rep'), 'head'), parts along dimension 0, may hold values from -23.069359 to 23.069359
- key: bfloat16 [4096, 1024], P(('groups', 'ctx'), 'head'), parts along dimension 0, may hold values from -6 to 6
- value: bfloat16 [4096, 1024], P(('groups', 'ctx'), 'head'), parts along dimension 0, may hold values from -24 to 24
- out_weight: bfloat16 [4096, 4096], P('head'), may hold values from -0.375 to 0.375
- cotangent: bfloat16 [2048, 4096], P(('groups', 'ctx', 'rep')), parts along dimension 0, may hold values from -6 to 6
- response: int32 [2048], P(('groups', 'ctx', 'rep')), parts along dimension 0, may hold values 0 or 1
- segment_ids: int32 [4096], P(('groups', 'ctx')), parts along dimension 0, may hold values from 0 to 31, never falling along the last dimension, each value on 1 to 128 neighbouring positions
- masked_segments: int32 [8], P('groups'), parts along dimension 0, may hold values from 0 to 31
Outputs:
- patch_effect: bfloat16 [2048, 4096], P(('groups', 'ctx', 'rep'), 'head'), parts along dimension 0
- token_attr: float32 [4096], P(('groups', 'ctx')), parts along dimension 0
- segment_attr: float32 [64], P('groups'), parts along dimension 0
There are 2 independent parts, one for each index of `groups`. A program takes and returns all parts, laid end to end along the dimension named above; an argument that names none is the same for every part. Nothing has to cross between parts.
All inputs are finite; a program needn't handle non-finite values. No bound on the sum of `response` on one device may be relied on, other than what follows from the above.
Results may differ from a plain program's by a relative error of at most 0.0095.
Values may be sent and summed in bfloat16 or wider, within the bound.
No kernel may reach another device: no remote copies, remote signals or barrier semaphores. Data moves between devices by JAX's collectives and lax.ppermute only.
A program may use at most 128 MiB of HBM per device.

v0:
```python
from functools import partial
import jax
import jax.numpy as jnp
from jax import lax
from jax.sharding import PartitionSpec as P

HD = 128
SEG_DEV = 8
NEG_FILL = -1e30


def split_heads(incoming):
    return incoming.reshape(incoming.shape[0], -1, HD)


def block_scores(query_rows, key_block):
    raw_scores = jnp.einsum(
        "gqd,tgd->gqt", query_rows, split_heads(key_block), preferred_element_type=jnp.float32
    )
    return raw_scores * HD ** (-0.5)


def visible_keys(row_pos, first_key, key_rows):
    key_pos = first_key + jnp.arange(key_rows, dtype=jnp.int32)
    return key_pos[None, None, :] <= row_pos[None, :, None]


def online_update(running, scores, allowed, value_heads):
    row_top, row_total, weighted = running
    chosen = jnp.where(allowed, scores, NEG_FILL)
    new_top = jnp.maximum(row_top, jnp.max(chosen, axis=2))
    shrink = jnp.exp(row_top - new_top)
    weights = jnp.where(allowed, jnp.exp(chosen - new_top[:, :, None]), 0.0)
    row_total = row_total * shrink + jnp.sum(weights, axis=2)
    weighted = weighted * shrink[:, :, None] + jnp.einsum(
        "gqt,tgd->gqd",
        weights.astype(jnp.bfloat16),
        value_heads,
        preferred_element_type=jnp.float32,
    )
    return (new_top, row_total, weighted)


def forward_piece(query_rows, row_pos, running, incoming, first_key):
    key_block, value_block, kept_flag = incoming
    scores = block_scores(query_rows, key_block)
    visible = visible_keys(row_pos, first_key, key_block.shape[0])
    kept_visible = jnp.logical_and(visible, kept_flag[None, None, :] > 0)
    value_heads = split_heads(value_block)
    return (
        online_update(running[0], scores, visible, value_heads),
        online_update(running[1], scores, kept_visible, value_heads),
    )


def backward_terms(
    query_rows, row_pos, grad_rows, log_total, row_dot, key_block, value_block, first_key
):
    scores = block_scores(query_rows, key_block)
    visible = visible_keys(row_pos, first_key, key_block.shape[0])
    shifted = jnp.where(visible, scores - log_total[:, :, None], 0.0)
    probability = jnp.where(visible, jnp.exp(shifted), 0.0)
    grad_prob = jnp.einsum(
        "gqd,tgd->gqt", grad_rows, split_heads(value_block), preferred_element_type=jnp.float32
    )
    return jnp.sum(
        probability * (grad_prob + (grad_prob - row_dot[:, :, None]) * shifted), axis=(0, 1)
    )


def blockwise(stepper, state_in, incoming, block_rows):
    length = jax.tree.leaves(incoming)[0].shape[0]

    def advance(counter, state_now):
        offset = counter * block_rows
        portion = jax.tree.map(
            lambda member: lax.dynamic_slice_in_dim(member, offset, block_rows, 0), incoming
        )
        return stepper(state_now, portion, offset)

    return lax.fori_loop(0, length // block_rows, advance, state_in)


def finish_pass(running):
    row_top, row_total, weighted = running
    return (weighted / row_total[:, :, None], row_top + jnp.log(row_total))


def local(query, key, value, out_weight, cotangent, response, segment_ids, masked_segments):
    ctx_count = lax.axis_size("ctx")
    rep_count = lax.axis_size("rep")
    ctx_at = lax.axis_index("ctx")
    rep_at = lax.axis_index("rep")
    query_count = query.shape[0]
    key_count = key.shape[0]
    kv_local = key.shape[1] // HD
    heads_local = query.shape[1] // HD
    group_size = heads_local // kv_local
    context_len = key_count * ctx_count
    query_base = context_len - query_count * ctx_count * rep_count
    row_width = group_size * query_count
    kept_flag = jnp.where(
        jnp.any(segment_ids[:, None] == masked_segments[None, :], axis=1), 0.0, 1.0
    ).astype(jnp.bfloat16)
    grad_masked = jnp.where(response[:, None] > 0, cotangent, jnp.zeros_like(cotangent))
    grad_out = jnp.dot(grad_masked, out_weight.T, preferred_element_type=jnp.float32).astype(
        jnp.bfloat16
    )

    def grouped(rows_in):
        return rows_in.reshape(query_count, kv_local, group_size, HD).transpose(1, 2, 0, 3)

    fresh_state = (
        jnp.full((kv_local, row_width), NEG_FILL, jnp.float32),
        jnp.zeros((kv_local, row_width), jnp.float32),
        jnp.zeros((kv_local, row_width, HD), jnp.float32),
    )
    starting = (fresh_state, fresh_state)
    query_rows = grouped(query).reshape(kv_local, row_width, HD)
    grad_own = grouped(grad_out).reshape(kv_local, row_width, HD)
    base_pos = (
        query_base
        + (ctx_at * rep_count + rep_at) * query_count
        + jnp.arange(query_count, dtype=jnp.int32)
    )
    own_pos = jnp.tile(base_pos, group_size)
    forward_step = partial(forward_piece, query_rows, own_pos)
    running = blockwise(
        forward_step,
        starting,
        (
            lax.all_gather(key, "ctx", axis=0, tiled=True),
            lax.all_gather(value, "ctx", axis=0, tiled=True),
            lax.all_gather(kept_flag, "ctx", axis=0, tiled=True),
        ),
        key_count,
    )
    clean_out, log_total = finish_pass(running[0])
    masked_out, _ = finish_pass(running[1])
    row_dot = jnp.sum(grad_own.astype(jnp.float32) * clean_out, axis=2)

    def backward_step(total_now, incoming, first_key):
        added = backward_terms(
            query_rows, own_pos, grad_own, log_total, row_dot, incoming[0], incoming[1], first_key
        )
        current = lax.dynamic_slice_in_dim(total_now, first_key, incoming[0].shape[0], 0)
        return lax.dynamic_update_slice_in_dim(total_now, current + added, first_key, 0)

    empty_attr = jnp.zeros((context_len,), jnp.float32)
    attr_all = blockwise(
        backward_step,
        empty_attr,
        (
            lax.all_gather(key, "ctx", axis=0, tiled=True),
            lax.all_gather(value, "ctx", axis=0, tiled=True),
        ),
        key_count,
    )
    local_attr = lax.psum_scatter(attr_all, "ctx", scatter_dimension=0, tiled=True)
    change = (
        (masked_out - clean_out)
        .reshape(kv_local, group_size, query_count, HD)
        .transpose(2, 0, 1, 3)
        .reshape(query_count, heads_local * HD)
        .astype(jnp.bfloat16)
    )
    projected = jnp.dot(change, out_weight, preferred_element_type=jnp.float32)
    patch_effect = lax.psum_scatter(projected, "head", scatter_dimension=1, tiled=True).astype(
        jnp.bfloat16
    )
    token_attr = lax.psum(local_attr, ("head", "rep"))
    onehot = (
        segment_ids[:, None] == jnp.arange(SEG_DEV * ctx_count, dtype=jnp.int32)[None, :]
    ).astype(jnp.float32)
    segment_attr = lax.psum(jnp.dot(token_attr, onehot, precision=lax.Precision.HIGHEST), "ctx")
    return (patch_effect, token_attr, segment_attr)


def solution(mesh):
    return jax.shard_map(
        local,
        mesh=mesh,
        in_specs=(
            P(("groups", "ctx", "rep"), "head"),
            P(("groups", "ctx"), "head"),
            P(("groups", "ctx"), "head"),
            P("head", None),
            P(("groups", "ctx", "rep"), None),
            P(("groups", "ctx", "rep")),
            P(("groups", "ctx")),
            P("groups"),
        ),
        out_specs=(P(("groups", "ctx", "rep"), "head"), P(("groups", "ctx")), P("groups")),
        check_vma=False,
    )
```

profile of v0, /device:TPU:0, one launch (start us, length us, event | category | flops | bytes accessed | tf_op | source)
XLA Modules:
  0.0 224.0 jit_solution(5980120812336782876)
XLA Ops:
  7.3 2.1 copy.57
  9.5 2.0 copy.59
  11.6 1.4 reshape.201
  13.3 13.7 %all-gather = bf16[4,1,512]{2,1,0:T(2,128)(2,1)S(1)} all-gather(bf16[1,1,512]{2,1,0:T(2,128)(2,1)S(1)} %reshape.205), channel_id=1, replica_groups=mesh['groups'=2,'ctx'=4,'head'=2,'rep'=2] {'ctx'}, dimensions={0}, use_global_device_ids=true | all-gather | bytes 5120 | tf_op jit(solution)/shard_map/all_gather | solution.py:134
  27.1 11.5 %convolution_convert_fusion = bf16[128,2048]{1,0:T(8,128)(2,1)S(1)} fusion(bf16[2048,4096]{1,0:T(8,128)(2,1)} %param.15, bf16[128,4096]{1,0:T(8,128)(2,1)S(1)} %copy-done.3, pred[128]{0:T(512)(128)(4,1)S(1)} %broadcast_compare_fusion.2), kind=kOutput, calls=%fused_computation.53 | convolution fusion | flops 2148270080 | bytes 18350208 | tf_op jit(solution)/shard_map/dot_general | solution.py:106
  40.5 18.3 %all-gather.4.cloned.1.call-done = bf16[2048,512]{0,1:T(8,128)(2,1)} async-done(((bf16[512,512]{0,1:T(8,128)(2,1)}), bf16[2048,512]{0,1:T(8,128)(2,1)}) %all-gather.4.cloned.1.call-update) | async-done | bytes 2097168 | tf_op jit(solution)/shard_map/all_gather | solution.py:132
  58.9 46.4 %all-gather.6.cloned.1.call-done = bf16[2048,512]{0,1:T(8,128)(2,1)} async-done(((bf16[512,512]{0,1:T(8,128)(2,1)}), bf16[2048,512]{0,1:T(8,128)(2,1)}) %all-gather.6.cloned.1.call-update) | async-done | bytes 2097168 | tf_op jit(solution)/shard_map/all_gather | solution.py:133
  105.2 54.5 %while.39 = (s32[]{:T(128)}, f32[4,512]{1,0:T(4,128)S(1)}, f32[4,512]{1,0:T(4,128)S(1)}, f32[4,512,128]{2,1,0:T(8,128)S(1)}, f32[4,512]{1,0:T(4,128)S(1)}, /*ind...) while((s32[]{:T(128)}, f32[4,512]{1,0:T(4,128)S(1)}, ...), condition=%wide.region_6.7_spmd.clone, body=%wide.region_1.6_spmd.clone.sunk | while | flops 832591872 | bytes 52702004 | solution.py:81
  105.6 1.1 constant_dynamic-slice_fusion.8
  106.7 3.4 %fusion.81 = (f32[4,512]{1,0:T(4,128)S(1)}, f32[4,512]{1,0:T(4,128)S(1)}, f32[4,512,512]{2,1,0:T(8,128)}) fusion(pred[512,512]{0,1:T(8,128)(4,1)S(1)} %get-tuple-element.631, pred[512,512]{0,1:T(8,128)(4,1)S(1)} %get-tuple-element.632, bf16[512,4,128]{0,2,1:T(8,128)(2,1)S(1)} %bitcast.121, bf16[4,512,128]{2,1,0:T(8,128)(2,1)S(1)} %get-tuple-element.682), kind=kOutput, calls=%fused_computation.19.clone.1 | convolution fusion | flops 273674240 | bytes 5783552 | tf_op jit(solution)/shard_map/while/body/eval_jaxpr/gqd,tgd->gqt/dot_general | solution.py:17
  110.1 3.7 %fusion.82 = (f32[4,512]{1,0:T(4,128)S(1)}, f32[4,512]{1,0:T(4,128)S(1)}) fusion(f32[4,512,512]{2,1,0:T(8,128)} %get-tuple-element.634, f32[4,512]{1,0:T(4,128)S(1)} %select_maximum_fusion.5, pred[512,512]{0,1:T(8,128)(4,1)S(1)} %get-tuple-element.631, f32[4,512]{1,0:T(4,128)S(1)} %select_maximum_fusion.4, pred[512,512]{0,1:T(8,128)(4,1)S(1)} %get-tuple-element.632), kind=kLoop, calls=%fused_computation.23.clone.1 | loop fusion | flops 9433088 | bytes 4751360 | tf_op jit(solution)/shard_map/while/body/eval_jaxpr/reduce_sum | solution.py:34
  113.9 1.1 constant_dynamic-slice_fusion.9
  115.0 1.9 fusion.85
  116.9 1.9 fusion.84
  119.3 1.1 constant_dynamic-slice_fusion.8
  120.4 3.4 %fusion.81 = (f32[4,512]{1,0:T(4,128)S(1)}, f32[4,512]{1,0:T(4,128)S(1)}, f32[4,512,512]{2,1,0:T(8,128)}) fusion(pred[512,512]{0,1:T(8,128)(4,1)S(1)} %get-tuple-element.631, pred[512,512]{0,1:T(8,128)(4,1)S(1)} %get-tuple-element.632, bf16[512,4,128]{0,2,1:T(8,128)(2,1)S(1)} %bitcast.121, bf16[4,512,128]{2,1,0:T(8,128)(2,1)S(1)} %get-tuple-element.682), kind=kOutput, calls=%fused_computation.19.clone.1 | convolution fusion | flops 273674240 | bytes 5783552 | tf_op jit(solution)/shard_map/while/body/eval_jaxpr/gqd,tgd->gqt/dot_general | solution.py:17
  123.8 3.7 %fusion.82 = (f32[4,512]{1,0:T(4,128)S(1)}, f32[4,512]{1,0:T(4,128)S(1)}) fusion(f32[4,512,512]{2,1,0:T(8,128)} %get-tuple-element.634, f32[4,512]{1,0:T(4,128)S(1)} %select_maximum_fusion.5, pred[512,512]{0,1:T(8,128)(4,1)S(1)} %get-tuple-element.631, f32[4,512]{1,0:T(4,128)S(1)} %select_maximum_fusion.4, pred[512,512]{0,1:T(8,128)(4,1)S(1)} %get-tuple-element.632), kind=kLoop, calls=%fused_computation.23.clone.1 | loop fusion | flops 9433088 | bytes 4751360 | tf_op jit(solution)/shard_map/while/body/eval_jaxpr/reduce_sum | solution.py:34
  127.5 1.1 constant_dynamic-slice_fusion.9
  128.6 1.9 fusion.85
  130.6 1.9 fusion.84
  132.9 1.1 constant_dynamic-slice_fusion.8
  134.0 3.4 %fusion.81 = (f32[4,512]{1,0:T(4,128)S(1)}, f32[4,512]{1,0:T(4,128)S(1)}, f32[4,512,512]{2,1,0:T(8,128)}) fusion(pred[512,512]{0,1:T(8,128)(4,1)S(1)} %get-tuple-element.631, pred[512,512]{0,1:T(8,128)(4,1)S(1)} %get-tuple-element.632, bf16[512,4,128]{0,2,1:T(8,128)(2,1)S(1)} %bitcast.121, bf16[4,512,128]{2,1,0:T(8,128)(2,1)S(1)} %get-tuple-element.682), kind=kOutput, calls=%fused_computation.19.clone.1 | convolution fusion | flops 273674240 | bytes 5783552 | tf_op jit(solution)/shard_map/while/body/eval_jaxpr/gqd,tgd->gqt/dot_general | solution.py:17
  137.4 3.7 %fusion.82 = (f32[4,512]{1,0:T(4,128)S(1)}, f32[4,512]{1,0:T(4,128)S(1)}) fusion(f32[4,512,512]{2,1,0:T(8,128)} %get-tuple-element.634, f32[4,512]{1,0:T(4,128)S(1)} %select_maximum_fusion.5, pred[512,512]{0,1:T(8,128)(4,1)S(1)} %get-tuple-element.631, f32[4,512]{1,0:T(4,128)S(1)} %select_maximum_fusion.4, pred[512,512]{0,1:T(8,128)(4,1)S(1)} %get-tuple-element.632), kind=kLoop, calls=%fused_computation.23.clone.1 | loop fusion | flops 9433088 | bytes 4751360 | tf_op jit(solution)/shard_map/while/body/eval_jaxpr/reduce_sum | solution.py:34
  141.2 1.1 constant_dynamic-slice_fusion.9
  142.3 1.9 fusion.85
  144.2 1.9 fusion.84
  146.6 1.1 constant_dynamic-slice_fusion.8
  147.7 3.4 %fusion.81 = (f32[4,512]{1,0:T(4,128)S(1)}, f32[4,512]{1,0:T(4,128)S(1)}, f32[4,512,512]{2,1,0:T(8,128)}) fusion(pred[512,512]{0,1:T(8,128)(4,1)S(1)} %get-tuple-element.631, pred[512,512]{0,1:T(8,128)(4,1)S(1)} %get-tuple-element.632, bf16[512,4,128]{0,2,1:T(8,128)(2,1)S(1)} %bitcast.121, bf16[4,512,128]{2,1,0:T(8,128)(2,1)S(1)} %get-tuple-element.682), kind=kOutput, calls=%fused_computation.19.clone.1 | convolution fusion | flops 273674240 | bytes 5783552 | tf_op jit(solution)/shard_map/while/body/eval_jaxpr/gqd,tgd->gqt/dot_general | solution.py:17
  151.1 3.7 %fusion.82 = (f32[4,512]{1,0:T(4,128)S(1)}, f32[4,512]{1,0:T(4,128)S(1)}) fusion(f32[4,512,512]{2,1,0:T(8,128)} %get-tuple-element.634, f32[4,512]{1,0:T(4,128)S(1)} %select_maximum_fusion.5, pred[512,512]{0,1:T(8,128)(4,1)S(1)} %get-tuple-element.631, f32[4,512]{1,0:T(4,128)S(1)} %select_maximum_fusion.4, pred[512,512]{0,1:T(8,128)(4,1)S(1)} %get-tuple-element.632), kind=kLoop, calls=%fused_computation.23.clone.1 | loop fusion | flops 9433088 | bytes 4751360 | tf_op jit(solution)/shard_map/while/body/eval_jaxpr/reduce_sum | solution.py:34
  154.8 1.1 constant_dynamic-slice_fusion.9
  155.9 1.9 fusion.85
  157.8 1.9 fusion.84
  159.8 2.1 multiply_reduce_fusion
  162.2 9.5 %fusion.39 = f32[128,4096]{1,0:T(8,128)} fusion(bf16[128,2048]{0,1:T(8,128)(2,1)S(1)} %bitcast.122, bf16[2048,4096]{1,0:T(8,128)(2,1)} %param.15), kind=kOutput, calls=%fused_computation.70 | convolution fusion | flops 2147483648 | bytes 19398656 | tf_op jit(solution)/shard_map/dot_general | solution.py:167
  171.8 18.3 %while.38 = (s32[]{:T(128)}, f32[2048]{0:T(1024)S(1)}, bf16[2048,512]{0,1:T(8,128)(2,1)}, bf16[4,512,128]{2,1,0:T(8,128)(2,1)S(1)}, f32[4,512]{1,0:T(4,128)S(1)}...) while((s32[]{:T(128)}, f32[2048]{0:T(1024)S(1)}, ...), condition=%wide.region_11.12_spmd.clone, body=%wide.region_9.11_spmd.clone.sunk | while | flops 546570752 | bytes 13140663 | solution.py:81
  171.8 1.3 constant_dynamic-slice_fusion.7
  173.1 0.7 fusion.73
  174.0 2.1 fusion.74
  176.3 1.5 constant_dynamic-slice_fusion.7
  178.7 2.1 fusion.74
  181.0 1.3 constant_dynamic-slice_fusion.7
  183.2 2.1 fusion.74
  185.5 1.3 constant_dynamic-slice_fusion.7
  187.7 2.1 fusion.74
  190.0 9.4 %all-reduce = f32[2048]{0:T(1024)S(1)} all-reduce(f32[2048]{0:T(1024)S(1)} %get-tuple-element.365), channel_id=3, replica_groups=mesh['groups'=2,'ctx'=4,'head'=2,'rep'=2] {'ctx'}, use_global_device_ids=true, to_apply=%region_12.13.clone | all-reduce | flops 2048 | bytes 16384
  199.5 5.6 %psum.14 = f32[512]{0:T(512)S(1)} all-reduce(f32[512]{0:T(512)S(1)} %dynamic-slice.1), channel_id=1, replica_groups=mesh['groups'=2,'ctx'=4,'head'=2,'rep'=2] {'head','rep'}, use_global_device_ids=true, to_apply=%region_13.14 | all-reduce | flops 512 | bytes 4096 | tf_op jit(solution)/shard_map/psum | solution.py:171
  205.4 10.0 %psum.15 = f32[32]{0:T(128)} all-reduce(f32[32]{0:T(128)S(1)} %convolution_bitcast_fusion), channel_id=1, replica_groups=mesh['groups'=2,'ctx'=4,'head'=2,'rep'=2] {'ctx'}, use_global_device_ids=true, to_apply=%region_14.15 | all-reduce | flops 32 | bytes 256 | tf_op jit(solution)/shard_map/psum | solution.py:175
  215.4 2.1 convert_element_type.44
  (120 shorter events, 7.9 us)
Async XLA Ops:
  7.2 6.0 %copy-start.4 = (s32[512]{0:T(512)S(1)}, s32[512]{0:T(512)}, u32[]{:S(2)}) copy-start(s32[512]{0:T(512)} %param.18) | copy-start | bytes 6148
  7.2 6.0 %copy-start.6 = (s32[4]{0:T(128)S(1)}, s32[4]{0:T(128)}, u32[]{:S(2)}) copy-start(s32[4]{0:T(128)} %param.19) | copy-start | bytes 52
  7.2 19.9 %copy-start.7 = (s32[128]{0:T(128)S(1)}, s32[128]{0:T(128)}, u32[]{:S(2)}) copy-start(s32[128]{0:T(128)} %param.17) | copy-start | bytes 1540
  7.2 19.9 %copy-start.3 = (bf16[128,4096]{1,0:T(8,128)(2,1)S(1)}, bf16[128,4096]{1,0:T(8,128)(2,1)}, u32[]{:S(2)}) copy-start(bf16[128,4096]{1,0:T(8,128)(2,1)} %param.16) | copy-start | bytes 3145732
  7.2 51.7 %all-gather.4.cloned.1.call-start = ((), (), s32[]{:S(2)}) async-start(), calls=%async_computation.1 | async-start | bytes 2621440 | tf_op jit(solution)/shard_map/all_gather | solution.py:132
  9.4 95.8 %all-gather.6.cloned.1.call-start = ((), (), s32[]{:S(2)}) async-start(), calls=%async_computation.2 | async-start | bytes 2621440 | tf_op jit(solution)/shard_map/all_gather | solution.py:133
  11.5 203.9 %reduce-scatter.2.cloned.1.call-start = ((), (), s32[]{:S(2)}) async-start(), calls=%async_computation.3 | async-start | bytes 3145728 | tf_op jit(solution)/shard_map/reduce_scatter | solution.py:168
  27.1 12.1 %copy-start.8 = (u32[32]{0:T(128)S(1)}, u32[32]{0:T(128)}, u32[]{:S(2)}) copy-start(u32[32]{0:T(128)} %constant.131) | copy-start | bytes 388
  110.1 4.9 %copy-start = (f32[4,512,512]{2,1,0:T(8,128)S(1)}, f32[4,512,512]{2,1,0:T(8,128)}, u32[]{:S(2)}) copy-start(f32[4,512,512]{2,1,0:T(8,128)} %get-tuple-element.634) | copy-start | bytes 12582916 | tf_op jit(solution)/shard_map/while
  110.1 4.9 %copy-start.1 = (f32[4,512,128]{2,1,0:T(8,128)S(1)}, f32[4,512,128]{2,1,0:T(8,128)}, u32[]{:S(2)}) copy-start(f32[4,512,128]{2,1,0:T(8,128)} %get-tuple-element.664) | copy-start | bytes 3145732 | tf_op jit(solution)/shard_map/while
  116.9 1.9 copy-start.2
  123.8 4.9 %copy-start = (f32[4,512,512]{2,1,0:T(8,128)S(1)}, f32[4,512,512]{2,1,0:T(8,128)}, u32[]{:S(2)}) copy-start(f32[4,512,512]{2,1,0:T(8,128)} %get-tuple-element.634) | copy-start | bytes 12582916 | tf_op jit(solution)/shard_map/while
  123.8 4.9 %copy-start.1 = (f32[4,512,128]{2,1,0:T(8,128)S(1)}, f32[4,512,128]{2,1,0:T(8,128)}, u32[]{:S(2)}) copy-start(f32[4,512,128]{2,1,0:T(8,128)} %get-tuple-element.664) | copy-start | bytes 3145732 | tf_op jit(solution)/shard_map/while
  130.6 1.9 copy-start.2
  137.4 4.9 %copy-start = (f32[4,512,512]{2,1,0:T(8,128)S(1)}, f32[4,512,512]{2,1,0:T(8,128)}, u32[]{:S(2)}) copy-start(f32[4,512,512]{2,1,0:T(8,128)} %get-tuple-element.634) | copy-start | bytes 12582916 | tf_op jit(solution)/shard_map/while
  137.4 4.9 %copy-start.1 = (f32[4,512,128]{2,1,0:T(8,128)S(1)}, f32[4,512,128]{2,1,0:T(8,128)}, u32[]{:S(2)}) copy-start(f32[4,512,128]{2,1,0:T(8,128)} %get-tuple-element.664) | copy-start | bytes 3145732 | tf_op jit(solution)/shard_map/while
  144.2 1.9 copy-start.2
  151.0 4.9 %copy-start = (f32[4,512,512]{2,1,0:T(8,128)S(1)}, f32[4,512,512]{2,1,0:T(8,128)}, u32[]{:S(2)}) copy-start(f32[4,512,512]{2,1,0:T(8,128)} %get-tuple-element.634) | copy-start | bytes 12582916 | tf_op jit(solution)/shard_map/while
  151.0 4.9 %copy-start.1 = (f32[4,512,128]{2,1,0:T(8,128)S(1)}, f32[4,512,128]{2,1,0:T(8,128)}, u32[]{:S(2)}) copy-start(f32[4,512,128]{2,1,0:T(8,128)} %get-tuple-element.664) | copy-start | bytes 3145732 | tf_op jit(solution)/shard_map/while
  157.8 1.9 copy-start.2
  205.1 12.4 %copy-start.5 = (f32[512]{0:T(512)}, f32[512]{0:T(512)S(1)}, u32[]{:S(2)}) copy-start(f32[512]{0:T(512)S(1)} %psum.14) | copy-start | bytes 6148
Sparse Core Ops, SparseCore 0:
  10.2 48.6 all-gather.3
  60.4 44.7 all-gather.5
  171.9 30.5 reduce-scatter.1
where the time goes:
time: 225 us; the launch traced here: 224 us
  waiting for transfers between devices  64.7 us (29%)
  matrix products  61.2 us (27%)
  blocking collectives  38.7 us (17%)
  other arithmetic  22.6 us (10%)
  local copies, waits for them, and re-layouts  21.4 us (10%)
  between operations  14.7 us (7%)
    all_gather x1, waiting for transfers between devices, local(): lax.all_gather(value, 'ctx', axis=0, tiled=True)  46.4 us
    all_gather x1, waiting for transfers between devices, local(): lax.all_gather(key, 'ctx', axis=0, tiled=True)  18.3 us
    dot_general x8, matrix products, block_scores(): jnp.einsum('gqd,tgd->gqt', query_rows, split_heads(key_block), preferred_...  16.3 us
    dot_general x8, matrix products, online_update(): jnp.einsum('gqt,tgd->gqd', weights.astype(jnp.bfloat16), value_heads, pre...  15.3 us
    reduce_sum x4, other arithmetic, online_update(): row_total = row_total * shrink + jnp.sum(weights, axis=2)  14.8 us
    dynamic_slice x12, local copies, waits for them, and re-layouts, advance(): lax.dynamic_slice_in_dim(member, offset, block_rows, 0)  14 us
    all_gather x1, blocking collectives, local(): lax.all_gather(kept_flag, 'ctx', axis=0, tiled=True)  13.7 us
    dot_general x1, matrix products, local(): jnp.dot(grad_masked, out_weight.T, preferred_element_type=jnp.float32)  11.5 us
  transfers between devices with their start and end apart: 3, of which 2 were waited for; matrix products, arithmetic and copies ran while one was open for 16% of the time, Pallas kernels for 0%

commit v1 on v0

--- a/solution.py
+++ b/solution.py
@@ -3,6 +3,7 @@
 import jax.numpy as jnp
 from jax import lax
 from jax.sharding import PartitionSpec as P
+from jax.lax import psum
 
 HD = 128
 SEG_DEV = 8
@@ -168,7 +169,8 @@
     patch_effect = lax.psum_scatter(projected, "head", scatter_dimension=1, tiled=True).astype(
         jnp.bfloat16
     )
-    token_attr = lax.psum(local_attr, ("head", "rep"))
+    end_sections_here = lambda inner_x, row_axis, net_axis: psum(psum(inner_x, row_axis), net_axis)
+    token_attr = end_sections_here(local_attr, "rep", "head")
     onehot = (
         segment_ids[:, None] == jnp.arange(SEG_DEV * ctx_count, dtype=jnp.int32)[None, :]
     ).astype(jnp.float32)

time: 225 us -> 227 us (level)
    psum x1 -> x2, blocking collectives: 5.63 us -> 7.36 us  [the longest x1 4.92 us: local(): psum(psum(inner_x, row_axis), net_axis)]
  transfers between devices with their start and end apart: 3 -> 3, of which waited for: 2 -> 2; matrix products, arithmetic and copies ran while one was open for 16% -> 15% of each run, Pallas kernels for 0% -> 0%
where the time goes in v1:
time: 227 us; the launch traced here: 226 us
  waiting for transfers between devices  64.7 us (29%)
  matrix products  61.3 us (27%)
  blocking collectives  40.4 us (18%)
  other arithmetic  22.6 us (10%)
  local copies, waits for them, and re-layouts  21.4 us (9%)
  between operations  14.7 us (6%)
    all_gather x1, waiting for transfers between devices, local(): lax.all_gather(value, 'ctx', axis=0, tiled=True)  46.4 us
    all_gather x1, waiting for transfers between devices, local(): lax.all_gather(key, 'ctx', axis=0, tiled=True)  18.3 us
    dot_general x8, matrix products, block_scores(): jnp.einsum('gqd,tgd->gqt', query_rows, split_heads(key_block), preferred_...  16.3 us
    dot_general x8, matrix products, online_update(): jnp.einsum('gqt,tgd->gqd', weights.astype(jnp.bfloat16), value_heads, pre...  15.3 us
    reduce_sum x4, other arithmetic, online_update(): row_total = row_total * shrink + jnp.sum(weights, axis=2)  14.8 us
    dynamic_slice x12, local copies, waits for them, and re-layouts, advance(): lax.dynamic_slice_in_dim(member, offset, block_rows, 0)  14 us
    all_gather x1, blocking collectives, local(): lax.all_gather(kept_flag, 'ctx', axis=0, tiled=True)  13.7 us
    dot_general x1, matrix products, local(): jnp.dot(grad_masked, out_weight.T, preferred_element_type=jnp.float32)  11.5 us
  transfers between devices with their start and end apart: 3, of which 2 were waited for; matrix products, arithmetic and copies ran while one was open for 15% of the time, Pallas kernels for 0%

profile of v1, /device:TPU:0, one launch (start us, length us, event | category | flops | bytes accessed | tf_op | source)
XLA Modules:
  0.0 225.8 jit_solution(934154797035908858)
XLA Ops:
  7.3 2.1 copy.57
  9.5 2.0 copy.59
  11.6 1.4 reshape.201
  13.3 13.7 %all-gather = bf16[4,1,512]{2,1,0:T(2,128)(2,1)S(1)} all-gather(bf16[1,1,512]{2,1,0:T(2,128)(2,1)S(1)} %reshape.205), channel_id=1, replica_groups=mesh['groups'=2,'ctx'=4,'head'=2,'rep'=2] {'ctx'}, dimensions={0}, use_global_device_ids=true | all-gather | bytes 5120 | tf_op jit(solution)/shard_map/all_gather | solution.py:135
  27.1 11.5 %convolution_convert_fusion = bf16[128,2048]{1,0:T(8,128)(2,1)S(1)} fusion(bf16[2048,4096]{1,0:T(8,128)(2,1)} %param.15, bf16[128,4096]{1,0:T(8,128)(2,1)S(1)} %copy-done.3, pred[128]{0:T(512)(128)(4,1)S(1)} %broadcast_compare_fusion.2), kind=kOutput, calls=%fused_computation.53 | convolution fusion | flops 2148270080 | bytes 18350208 | tf_op jit(solution)/shard_map/dot_general | solution.py:107
  40.5 18.3 %all-gather.4.cloned.1.call-done = bf16[2048,512]{0,1:T(8,128)(2,1)} async-done(((bf16[512,512]{0,1:T(8,128)(2,1)}), bf16[2048,512]{0,1:T(8,128)(2,1)}) %all-gather.4.cloned.1.call-update) | async-done | bytes 2097168 | tf_op jit(solution)/shard_map/all_gather | solution.py:133
  58.9 46.4 %all-gather.6.cloned.1.call-done = bf16[2048,512]{0,1:T(8,128)(2,1)} async-done(((bf16[512,512]{0,1:T(8,128)(2,1)}), bf16[2048,512]{0,1:T(8,128)(2,1)}) %all-gather.6.cloned.1.call-update) | async-done | bytes 2097168 | tf_op jit(solution)/shard_map/all_gather | solution.py:134
  105.2 54.5 %while.39 = (s32[]{:T(128)}, f32[4,512]{1,0:T(4,128)S(1)}, f32[4,512]{1,0:T(4,128)S(1)}, f32[4,512,128]{2,1,0:T(8,128)S(1)}, f32[4,512]{1,0:T(4,128)S(1)}, /*ind...) while((s32[]{:T(128)}, f32[4,512]{1,0:T(4,128)S(1)}, ...), condition=%wide.region_6.7_spmd.clone, body=%wide.region_1.6_spmd.clone.sunk | while | flops 832591872 | bytes 52702004 | solution.py:82
  105.6 1.1 constant_dynamic-slice_fusion.8
  106.7 3.4 %fusion.81 = (f32[4,512]{1,0:T(4,128)S(1)}, f32[4,512]{1,0:T(4,128)S(1)}, f32[4,512,512]{2,1,0:T(8,128)}) fusion(pred[512,512]{0,1:T(8,128)(4,1)S(1)} %get-tuple-element.631, pred[512,512]{0,1:T(8,128)(4,1)S(1)} %get-tuple-element.632, bf16[512,4,128]{0,2,1:T(8,128)(2,1)S(1)} %bitcast.121, bf16[4,512,128]{2,1,0:T(8,128)(2,1)S(1)} %get-tuple-element.682), kind=kOutput, calls=%fused_computation.19.clone.1 | convolution fusion | flops 273674240 | bytes 5783552 | tf_op jit(solution)/shard_map/while/body/eval_jaxpr/gqd,tgd->gqt/dot_general | solution.py:18
  110.1 3.7 %fusion.82 = (f32[4,512]{1,0:T(4,128)S(1)}, f32[4,512]{1,0:T(4,128)S(1)}) fusion(f32[4,512,512]{2,1,0:T(8,128)} %get-tuple-element.634, f32[4,512]{1,0:T(4,128)S(1)} %select_maximum_fusion.5, pred[512,512]{0,1:T(8,128)(4,1)S(1)} %get-tuple-element.631, f32[4,512]{1,0:T(4,128)S(1)} %select_maximum_fusion.4, pred[512,512]{0,1:T(8,128)(4,1)S(1)} %get-tuple-element.632), kind=kLoop, calls=%fused_computation.23.clone.1 | loop fusion | flops 9433088 | bytes 4751360 | tf_op jit(solution)/shard_map/while/body/eval_jaxpr/reduce_sum | solution.py:35
  113.9 1.1 constant_dynamic-slice_fusion.9
  115.0 1.9 fusion.85
  116.9 1.9 fusion.84
  119.3 1.1 constant_dynamic-slice_fusion.8
  120.4 3.4 %fusion.81 = (f32[4,512]{1,0:T(4,128)S(1)}, f32[4,512]{1,0:T(4,128)S(1)}, f32[4,512,512]{2,1,0:T(8,128)}) fusion(pred[512,512]{0,1:T(8,128)(4,1)S(1)} %get-tuple-element.631, pred[512,512]{0,1:T(8,128)(4,1)S(1)} %get-tuple-element.632, bf16[512,4,128]{0,2,1:T(8,128)(2,1)S(1)} %bitcast.121, bf16[4,512,128]{2,1,0:T(8,128)(2,1)S(1)} %get-tuple-element.682), kind=kOutput, calls=%fused_computation.19.clone.1 | convolution fusion | flops 273674240 | bytes 5783552 | tf_op jit(solution)/shard_map/while/body/eval_jaxpr/gqd,tgd->gqt/dot_general | solution.py:18
  123.8 3.7 %fusion.82 = (f32[4,512]{1,0:T(4,128)S(1)}, f32[4,512]{1,0:T(4,128)S(1)}) fusion(f32[4,512,512]{2,1,0:T(8,128)} %get-tuple-element.634, f32[4,512]{1,0:T(4,128)S(1)} %select_maximum_fusion.5, pred[512,512]{0,1:T(8,128)(4,1)S(1)} %get-tuple-element.631, f32[4,512]{1,0:T(4,128)S(1)} %select_maximum_fusion.4, pred[512,512]{0,1:T(8,128)(4,1)S(1)} %get-tuple-element.632), kind=kLoop, calls=%fused_computation.23.clone.1 | loop fusion | flops 9433088 | bytes 4751360 | tf_op jit(solution)/shard_map/while/body/eval_jaxpr/reduce_sum | solution.py:35
  127.5 1.1 constant_dynamic-slice_fusion.9
  128.6 1.9 fusion.85
  130.6 1.9 fusion.84
  132.9 1.1 constant_dynamic-slice_fusion.8
  134.0 3.4 %fusion.81 = (f32[4,512]{1,0:T(4,128)S(1)}, f32[4,512]{1,0:T(4,128)S(1)}, f32[4,512,512]{2,1,0:T(8,128)}) fusion(pred[512,512]{0,1:T(8,128)(4,1)S(1)} %get-tuple-element.631, pred[512,512]{0,1:T(8,128)(4,1)S(1)} %get-tuple-element.632, bf16[512,4,128]{0,2,1:T(8,128)(2,1)S(1)} %bitcast.121, bf16[4,512,128]{2,1,0:T(8,128)(2,1)S(1)} %get-tuple-element.682), kind=kOutput, calls=%fused_computation.19.clone.1 | convolution fusion | flops 273674240 | bytes 5783552 | tf_op jit(solution)/shard_map/while/body/eval_jaxpr/gqd,tgd->gqt/dot_general | solution.py:18
  137.4 3.7 %fusion.82 = (f32[4,512]{1,0:T(4,128)S(1)}, f32[4,512]{1,0:T(4,128)S(1)}) fusion(f32[4,512,512]{2,1,0:T(8,128)} %get-tuple-element.634, f32[4,512]{1,0:T(4,128)S(1)} %select_maximum_fusion.5, pred[512,512]{0,1:T(8,128)(4,1)S(1)} %get-tuple-element.631, f32[4,512]{1,0:T(4,128)S(1)} %select_maximum_fusion.4, pred[512,512]{0,1:T(8,128)(4,1)S(1)} %get-tuple-element.632), kind=kLoop, calls=%fused_computation.23.clone.1 | loop fusion | flops 9433088 | bytes 4751360 | tf_op jit(solution)/shard_map/while/body/eval_jaxpr/reduce_sum | solution.py:35
  141.2 1.1 constant_dynamic-slice_fusion.9
  142.3 1.9 fusion.85
  144.2 1.9 fusion.84
  146.6 1.1 constant_dynamic-slice_fusion.8
  147.7 3.4 %fusion.81 = (f32[4,512]{1,0:T(4,128)S(1)}, f32[4,512]{1,0:T(4,128)S(1)}, f32[4,512,512]{2,1,0:T(8,128)}) fusion(pred[512,512]{0,1:T(8,128)(4,1)S(1)} %get-tuple-element.631, pred[512,512]{0,1:T(8,128)(4,1)S(1)} %get-tuple-element.632, bf16[512,4,128]{0,2,1:T(8,128)(2,1)S(1)} %bitcast.121, bf16[4,512,128]{2,1,0:T(8,128)(2,1)S(1)} %get-tuple-element.682), kind=kOutput, calls=%fused_computation.19.clone.1 | convolution fusion | flops 273674240 | bytes 5783552 | tf_op jit(solution)/shard_map/while/body/eval_jaxpr/gqd,tgd->gqt/dot_general | solution.py:18
  151.1 3.7 %fusion.82 = (f32[4,512]{1,0:T(4,128)S(1)}, f32[4,512]{1,0:T(4,128)S(1)}) fusion(f32[4,512,512]{2,1,0:T(8,128)} %get-tuple-element.634, f32[4,512]{1,0:T(4,128)S(1)} %select_maximum_fusion.5, pred[512,512]{0,1:T(8,128)(4,1)S(1)} %get-tuple-element.631, f32[4,512]{1,0:T(4,128)S(1)} %select_maximum_fusion.4, pred[512,512]{0,1:T(8,128)(4,1)S(1)} %get-tuple-element.632), kind=kLoop, calls=%fused_computation.23.clone.1 | loop fusion | flops 9433088 | bytes 4751360 | tf_op jit(solution)/shard_map/while/body/eval_jaxpr/reduce_sum | solution.py:35
  154.8 1.1 constant_dynamic-slice_fusion.9
  155.9 1.9 fusion.85
  157.8 1.9 fusion.84
  159.8 2.1 multiply_reduce_fusion
  162.2 9.5 %fusion.39 = f32[128,4096]{1,0:T(8,128)} fusion(bf16[128,2048]{0,1:T(8,128)(2,1)S(1)} %bitcast.122, bf16[2048,4096]{1,0:T(8,128)(2,1)} %param.15), kind=kOutput, calls=%fused_computation.70 | convolution fusion | flops 2147483648 | bytes 19398656 | tf_op jit(solution)/shard_map/dot_general | solution.py:168
  171.8 18.3 %while.38 = (s32[]{:T(128)}, f32[2048]{0:T(1024)S(1)}, bf16[2048,512]{0,1:T(8,128)(2,1)}, bf16[4,512,128]{2,1,0:T(8,128)(2,1)S(1)}, f32[4,512]{1,0:T(4,128)S(1)}...) while((s32[]{:T(128)}, f32[2048]{0:T(1024)S(1)}, ...), condition=%wide.region_11.12_spmd.clone, body=%wide.region_9.11_spmd.clone.sunk | while | flops 546570752 | bytes 13140663 | solution.py:82
  171.8 1.3 constant_dynamic-slice_fusion.7
  174.0 2.1 fusion.74
  176.3 1.5 constant_dynamic-slice_fusion.7
  178.7 2.1 fusion.74
  181.1 1.3 constant_dynamic-slice_fusion.7
  183.3 2.1 fusion.74
  185.6 1.3 constant_dynamic-slice_fusion.7
  187.8 2.1 fusion.74
  190.1 9.4 %all-reduce = f32[2048]{0:T(1024)S(1)} all-reduce(f32[2048]{0:T(1024)S(1)} %get-tuple-element.365), channel_id=3, replica_groups=mesh['groups'=2,'ctx'=4,'head'=2,'rep'=2] {'ctx'}, use_global_device_ids=true, to_apply=%region_12.13.clone | all-reduce | flops 2048 | bytes 16384
  199.6 2.4 %psum.21 = f32[512]{0:T(512)S(1)} all-reduce(f32[512]{0:T(512)S(1)} %dynamic-slice.1), channel_id=1, replica_groups=mesh['groups'=2,'ctx'=4,'head'=2,'rep'=2] {'rep'}, use_global_device_ids=true, to_apply=%region_13.14 | all-reduce | flops 512 | bytes 4096 | tf_op jit(solution)/shard_map/psum | solution.py:172
  202.0 4.9 %psum.22 = f32[512]{0:T(512)S(1)} all-reduce(f32[512]{0:T(512)S(1)} %psum.21), channel_id=1, replica_groups=mesh['groups'=2,'ctx'=4,'head'=2,'rep'=2] {'head'}, use_global_device_ids=true, to_apply=%region_14.15 | all-reduce | flops 512 | bytes 4096 | tf_op jit(solution)/shard_map/psum | solution.py:172
  207.2 10.0 %psum.23 = f32[32]{0:T(128)} all-reduce(f32[32]{0:T(128)S(1)} %convolution_bitcast_fusion), channel_id=1, replica_groups=mesh['groups'=2,'ctx'=4,'head'=2,'rep'=2] {'ctx'}, use_global_device_ids=true, to_apply=%region_15.16 | all-reduce | flops 32 | bytes 256 | tf_op jit(solution)/shard_map/psum | solution.py:177
  217.2 2.1 convert_element_type.44
  (121 shorter events, 8.5 us)
Async XLA Ops:
  7.2 6.0 %copy-start.4 = (s32[512]{0:T(512)S(1)}, s32[512]{0:T(512)}, u32[]{:S(2)}) copy-start(s32[512]{0:T(512)} %param.18) | copy-start | bytes 6148
  7.2 6.0 %copy-start.6 = (s32[4]{0:T(128)S(1)}, s32[4]{0:T(128)}, u32[]{:S(2)}) copy-start(s32[4]{0:T(128)} %param.19) | copy-start | bytes 52
  7.2 19.9 %copy-start.7 = (s32[128]{0:T(128)S(1)}, s32[128]{0:T(128)}, u32[]{:S(2)}) copy-start(s32[128]{0:T(128)} %param.17) | copy-start | bytes 1540
  7.2 19.9 %copy-start.3 = (bf16[128,4096]{1,0:T(8,128)(2,1)S(1)}, bf16[128,4096]{1,0:T(8,128)(2,1)}, u32[]{:S(2)}) copy-start(bf16[128,4096]{1,0:T(8,128)(2,1)} %param.16) | copy-start | bytes 3145732
  7.2 51.7 %all-gather.4.cloned.1.call-start = ((), (), s32[]{:S(2)}) async-start(), calls=%async_computation.1 | async-start | bytes 2621440 | tf_op jit(solution)/shard_map/all_gather | solution.py:133
  9.4 95.8 %all-gather.6.cloned.1.call-start = ((), (), s32[]{:S(2)}) async-start(), calls=%async_computation.2 | async-start | bytes 2621440 | tf_op jit(solution)/shard_map/all_gather | solution.py:134
  11.5 205.7 %reduce-scatter.2.cloned.1.call-start = ((), (), s32[]{:S(2)}) async-start(), calls=%async_computation.3 | async-start | bytes 3145728 | tf_op jit(solution)/shard_map/reduce_scatter | solution.py:169
  27.1 12.1 %copy-start.8 = (u32[32]{0:T(128)S(1)}, u32[32]{0:T(128)}, u32[]{:S(2)}) copy-start(u32[32]{0:T(128)} %constant.131) | copy-start | bytes 388
  110.1 4.9 %copy-start = (f32[4,512,512]{2,1,0:T(8,128)S(1)}, f32[4,512,512]{2,1,0:T(8,128)}, u32[]{:S(2)}) copy-start(f32[4,512,512]{2,1,0:T(8,128)} %get-tuple-element.634) | copy-start | bytes 12582916 | tf_op jit(solution)/shard_map/while
  110.1 4.9 %copy-start.1 = (f32[4,512,128]{2,1,0:T(8,128)S(1)}, f32[4,512,128]{2,1,0:T(8,128)}, u32[]{:S(2)}) copy-start(f32[4,512,128]{2,1,0:T(8,128)} %get-tuple-element.664) | copy-start | bytes 3145732 | tf_op jit(solution)/shard_map/while
  116.9 1.9 copy-start.2
  123.8 4.9 %copy-start = (f32[4,512,512]{2,1,0:T(8,128)S(1)}, f32[4,512,512]{2,1,0:T(8,128)}, u32[]{:S(2)}) copy-start(f32[4,512,512]{2,1,0:T(8,128)} %get-tuple-element.634) | copy-start | bytes 12582916 | tf_op jit(solution)/shard_map/while
  123.8 4.9 %copy-start.1 = (f32[4,512,128]{2,1,0:T(8,128)S(1)}, f32[4,512,128]{2,1,0:T(8,128)}, u32[]{:S(2)}) copy-start(f32[4,512,128]{2,1,0:T(8,128)} %get-tuple-element.664) | copy-start | bytes 3145732 | tf_op jit(solution)/shard_map/while
  130.6 1.9 copy-start.2
  137.4 4.9 %copy-start = (f32[4,512,512]{2,1,0:T(8,128)S(1)}, f32[4,512,512]{2,1,0:T(8,128)}, u32[]{:S(2)}) copy-start(f32[4,512,512]{2,1,0:T(8,128)} %get-tuple-element.634) | copy-start | bytes 12582916 | tf_op jit(solution)/shard_map/while
  137.4 4.9 %copy-start.1 = (f32[4,512,128]{2,1,0:T(8,128)S(1)}, f32[4,512,128]{2,1,0:T(8,128)}, u32[]{:S(2)}) copy-start(f32[4,512,128]{2,1,0:T(8,128)} %get-tuple-element.664) | copy-start | bytes 3145732 | tf_op jit(solution)/shard_map/while
  144.2 1.9 copy-start.2
  151.0 4.9 %copy-start = (f32[4,512,512]{2,1,0:T(8,128)S(1)}, f32[4,512,512]{2,1,0:T(8,128)}, u32[]{:S(2)}) copy-start(f32[4,512,512]{2,1,0:T(8,128)} %get-tuple-element.634) | copy-start | bytes 12582916 | tf_op jit(solution)/shard_map/while
  151.0 4.9 %copy-start.1 = (f32[4,512,128]{2,1,0:T(8,128)S(1)}, f32[4,512,128]{2,1,0:T(8,128)}, u32[]{:S(2)}) copy-start(f32[4,512,128]{2,1,0:T(8,128)} %get-tuple-element.664) | copy-start | bytes 3145732 | tf_op jit(solution)/shard_map/while
  157.8 1.9 copy-start.2
  206.9 12.3 %copy-start.5 = (f32[512]{0:T(512)}, f32[512]{0:T(512)S(1)}, u32[]{:S(2)}) copy-start(f32[512]{0:T(512)S(1)} %psum.22) | copy-start | bytes 6148
Sparse Core Ops, SparseCore 0:
  10.2 48.6 all-gather.3
  60.4 44.7 all-gather.5
  171.9 30.5 reduce-scatter.1
